TPU v7x, 128 devices: a whole 4x4x4 slice. The times are simulated.
128 devices in a mesh: dp: 16 (over x, y), feat: 8 (over z, core).
Axes of the slice: x: 4, y: 4, z: 4, core: 2. Of those that a mesh axis runs over, the one named last changes fastest.
Arguments:
- images: bfloat16 [8192, 3072], P(('dp', 'feat')), may hold values from -6 to 6
- labels: int32 [8192], P('dp'), may hold values from 0 to 999
- predictions: float32 [8192, 1000], P('dp'), may hold values from -2 to 2
- filters: bfloat16 [75, 1024], P(None, 'feat'), may hold values from -0.75 to 0.75
- biases: float32 [1024], P('feat'), may hold values from -3 to 3
Outputs:
- weights: float32 [4096, 1000], P('feat')
- new_residual: float32 [8192, 1000], P(('dp', 'feat'))
All inputs are finite; a program needn't handle non-finite values.
Results may differ from a plain program's by a relative error of at most 0.007.
The roundings to bfloat16 on the way count: a program that leaves them out, or rounds other values in their place, can miss the bound.
Values may be sent and summed in bfloat16 or wider, within the bound.
No kernel may reach another device: no remote copies, remote signals or barrier semaphores. Data moves between devices by JAX's collectives and lax.ppermute only.
A program may use at most 192 MiB of HBM per device.

v0:
```python
import math
import jax
import jax.numpy as jnp
from jax import lax
from jax.sharding import PartitionSpec as P

SIDE = 32
CHAN = 3
KSIZE = 5


def chol_solve(factor, rhs):
    middle = lax.linalg.triangular_solve(factor, rhs, left_side=True, lower=True, transpose_a=False)
    return lax.linalg.triangular_solve(factor, middle, left_side=True, lower=True, transpose_a=True)


def split_parts(values):
    upper = values.astype(jnp.bfloat16)
    lower = (values - upper.astype(jnp.float32)).astype(jnp.bfloat16)
    return (upper, lower)


def left_product(feats, other):
    return lax.dot_general(
        feats, other, (((0,), (0,)), ((), ())), preferred_element_type=jnp.float32
    )


def conv_pool(imgs, kernel, offsets):
    count = imgs.shape[0]
    filt_count = kernel.shape[3]
    pics = imgs.reshape(count, SIDE, SIDE, CHAN)
    response = lax.conv_general_dilated(
        pics,
        kernel,
        (1, 1),
        "VALID",
        dimension_numbers=("NHWC", "HWIO", "NHWC"),
        preferred_element_type=jnp.float32,
    )
    response = jnp.maximum(response + offsets, 0.0)
    half = (SIDE - KSIZE + 1) // 2
    pooled = response.reshape(count, 2, half, 2, half, filt_count).mean(axis=(2, 4))
    return jnp.transpose(pooled, (0, 3, 1, 2)).reshape(count, 4 * filt_count).astype(jnp.bfloat16)


def shards(images, labels, predictions, filters, biases):
    filt_count = filters.shape[1]
    kernel = filters.reshape(KSIZE, KSIZE, CHAN, filt_count)
    share = images.shape[0]
    total_images = share * lax.axis_size("feat") * lax.axis_size("dp")
    piece = lax.all_gather(images, "feat", axis=0, tiled=True)
    count = piece.shape[0]
    group = math.gcd(count, 128)
    blocks = piece.reshape(count // group, group, piece.shape[1])
    out = lax.map(lambda part: conv_pool(part, kernel, biases), blocks)
    feats = out.reshape(count, 4 * filt_count)
    width = feats.shape[1]
    residual = (
        labels[:, None] == jnp.arange(predictions.shape[1], dtype=jnp.int32)[None, :]
    ).astype(jnp.float32) - predictions
    res_upper, res_lower = split_parts(residual)
    gram = lax.psum(left_product(feats, feats), "dp")
    cross = left_product(feats, res_upper) + left_product(feats, res_lower)
    cross, gram = lax.optimization_barrier((cross, gram))
    cross = lax.psum(cross, "dp")
    gram = gram / total_images + 0.5 * jnp.eye(width, dtype=jnp.float32)
    cross = cross / total_images
    factor = jnp.linalg.cholesky(gram)
    solved = chol_solve(factor, cross)
    sol_upper, sol_lower = split_parts(solved)
    fitted = lax.psum_scatter(
        (
            jnp.dot(feats, sol_upper, preferred_element_type=jnp.float32)
            + jnp.dot(feats, sol_lower, preferred_element_type=jnp.float32)
        ).astype(jnp.bfloat16),
        "feat",
        scatter_dimension=0,
        tiled=True,
    ).astype(jnp.float32)
    mine = lax.dynamic_slice_in_dim(residual, lax.axis_index("feat") * share, share, 0)
    return (solved, mine - fitted)


def solution(mesh):
    placed = (P(("dp", "feat"), None), P("dp"), P("dp", None), P(None, "feat"), P("feat"))
    return jax.shard_map(
        shards,
        mesh=mesh,
        in_specs=placed,
        out_specs=(P("feat", None), P(("dp", "feat"), None)),
        check_vma=False,
    )
```

profile of v0, /device:TPU:0, one launch (start us, length us, event | category | flops | bytes accessed | tf_op | source)
XLA Modules:
  0.0 528.2 jit_solution(10686514619989856401)
XLA Ops:
  8.0 0.7 reshape.78
  8.7 2.9 copy.22
  12.1 28.0 %all-gather.2.cloned.1.call-done = bf16[512,3072]{1,0:T(8,128)(2,1)} async-done(((bf16[64,3072]{1,0:T(8,128)(2,1)}), bf16[512,3072]{1,0:T(8,128)(2,1)}) %all-gather.2.cloned.1.call-update) | async-done | bytes 3145744 | tf_op jit(solution)/shard_map/all_gather | solution.py:52
  40.1 152.3 %while.11 = (s32[]{:T(128)}, bf16[4,128,512]{1,2,0:T(8,128)(2,1)}, bf16[4,128,3072]{2,1,0:T(8,128)(2,1)}, bf16[5,5,3,128]{3,2,1,0:T(4,128)(2,1)S(1)}, f32[128]{0:T(128)S(1)}, /*index=5*/s32[]{:T(128)}, f32[]{:T(128)}) while((s32[]{:T(128)}, bf16[4,128,512]{1,2,0:T(8,128)(2,1)}, bf16[4,128,3072]{2,1,0:T(8,128)(2,1)}, ...), condition=%wide.region_2.3_spmd, body=%wide.region_0.2_spmd.sunk | while | flops 1965359104 | bytes 109465424 | solution.py:56
  40.1 1.2 constant_dynamic-slice_fusion.4
  42.1 19.1 %add_maximum_fusion.2 = f32[128,28,28,128]{3,0,2,1:T(8,128)} fusion(f32[128]{0:T(128)S(1)} %get-tuple-element.169, bf16[128,32,32,3]{0,3,2,1:T(4,128)(2,1)S(1)} %reshape.101, bf16[5,5,3,128]{3,2,1,0:T(4,128)(2,1)S(1)} %get-tuple-element.168), kind=kOutput, calls=%fused_computation.clone.1 | convolution fusion | flops 1952448512 | bytes 52186368 | tf_op jit(solution)/shard_map/while/body/eval_jaxpr/conv_general_dilated | solution.py:33
  61.2 16.1 %reduce_sum.10 = f32[128,2,2,128]{3,0,2,1:T(8,128)S(1)} reduce(f32[128,2,14,2,14,128]{5,0,4,3,2,1:T(8,128)} %bitcast.85, f32[]{:T(128)} %constant.173.clone.1..sunk), dimensions={2,4}, to_apply=%region_1.1 | reduce | flops 12779520 | bytes 51642372 | tf_op jit(solution)/shard_map/while/body/eval_jaxpr/reduce_sum | solution.py:43
  78.2 1.2 constant_dynamic-slice_fusion.4
  80.1 19.1 %add_maximum_fusion.2 = f32[128,28,28,128]{3,0,2,1:T(8,128)} fusion(f32[128]{0:T(128)S(1)} %get-tuple-element.169, bf16[128,32,32,3]{0,3,2,1:T(4,128)(2,1)S(1)} %reshape.101, bf16[5,5,3,128]{3,2,1,0:T(4,128)(2,1)S(1)} %get-tuple-element.168), kind=kOutput, calls=%fused_computation.clone.1 | convolution fusion | flops 1952448512 | bytes 52186368 | tf_op jit(solution)/shard_map/while/body/eval_jaxpr/conv_general_dilated | solution.py:33
  99.3 16.1 %reduce_sum.10 = f32[128,2,2,128]{3,0,2,1:T(8,128)S(1)} reduce(f32[128,2,14,2,14,128]{5,0,4,3,2,1:T(8,128)} %bitcast.85, f32[]{:T(128)} %constant.173.clone.1..sunk), dimensions={2,4}, to_apply=%region_1.1 | reduce | flops 12779520 | bytes 51642372 | tf_op jit(solution)/shard_map/while/body/eval_jaxpr/reduce_sum | solution.py:43
  116.2 1.2 constant_dynamic-slice_fusion.4
  118.2 19.1 %add_maximum_fusion.2 = f32[128,28,28,128]{3,0,2,1:T(8,128)} fusion(f32[128]{0:T(128)S(1)} %get-tuple-element.169, bf16[128,32,32,3]{0,3,2,1:T(4,128)(2,1)S(1)} %reshape.101, bf16[5,5,3,128]{3,2,1,0:T(4,128)(2,1)S(1)} %get-tuple-element.168), kind=kOutput, calls=%fused_computation.clone.1 | convolution fusion | flops 1952448512 | bytes 52186368 | tf_op jit(solution)/shard_map/while/body/eval_jaxpr/conv_general_dilated | solution.py:33
  137.3 16.1 %reduce_sum.10 = f32[128,2,2,128]{3,0,2,1:T(8,128)S(1)} reduce(f32[128,2,14,2,14,128]{5,0,4,3,2,1:T(8,128)} %bitcast.85, f32[]{:T(128)} %constant.173.clone.1..sunk), dimensions={2,4}, to_apply=%region_1.1 | reduce | flops 12779520 | bytes 51642372 | tf_op jit(solution)/shard_map/while/body/eval_jaxpr/reduce_sum | solution.py:43
  154.3 1.2 constant_dynamic-slice_fusion.4
  156.3 19.1 %add_maximum_fusion.2 = f32[128,28,28,128]{3,0,2,1:T(8,128)} fusion(f32[128]{0:T(128)S(1)} %get-tuple-element.169, bf16[128,32,32,3]{0,3,2,1:T(4,128)(2,1)S(1)} %reshape.101, bf16[5,5,3,128]{3,2,1,0:T(4,128)(2,1)S(1)} %get-tuple-element.168), kind=kOutput, calls=%fused_computation.clone.1 | convolution fusion | flops 1952448512 | bytes 52186368 | tf_op jit(solution)/shard_map/while/body/eval_jaxpr/conv_general_dilated | solution.py:33
  175.4 16.1 %reduce_sum.10 = f32[128,2,2,128]{3,0,2,1:T(8,128)S(1)} reduce(f32[128,2,14,2,14,128]{5,0,4,3,2,1:T(8,128)} %bitcast.85, f32[]{:T(128)} %constant.173.clone.1..sunk), dimensions={2,4}, to_apply=%region_1.1 | reduce | flops 12779520 | bytes 51642372 | tf_op jit(solution)/shard_map/while/body/eval_jaxpr/reduce_sum | solution.py:43
  192.4 2.7 convolution_bitcast_fusion
  195.4 1.9 convert_subtract_fusion
  198.2 2.0 convolution_add_fusion
  200.3 82.0 %all-reduce.4.cloned.1.call-done = f32[512,512]{1,0:T(8,128)} async-done(((f32[512,512]{1,0:T(8,128)}), f32[512,512]{1,0:T(8,128)}) %all-reduce.4.cloned.1.call-update) | async-done | bytes 1048592 | tf_op jit(solution)/shard_map/psum | solution.py:63
  282.3 2.3 select_add_fusion
  284.6 2.6 copy.24
  287.2 1.8 fusion.19
  289.0 1.0 copy-done.3
  290.0 11.7 %cholesky.103 = f32[128,128]{1,0:T(8,128)S(1)} custom-call(f32[128,128]{1,0:T(8,128)S(1)} %cholesky.263), custom_call_target="Cholesky" | custom-call | tf_op jit(solution)/shard_map/jit(cholesky)/cholesky | solution.py:69
  301.7 1.1 cholesky.222
  302.8 9.8 %custom-call.32 = f32[1,128,128]{1,2,0:T(8,128)S(1)} custom-call(f32[1,128,128]{2,1,0:T(8,128)S(1)} %get-tuple-element.86), custom_call_target="InvertDiagBlocksLowerTriangular" | custom-call | tf_op jit(solution)/shard_map/jit(cholesky)/cholesky | solution.py:69
  312.6 2.0 constant_dynamic-update-slice_fusion.4
  314.6 1.3 convolution_subtract_fusion.4
  315.9 12.1 %cholesky.215 = f32[128,128]{1,0:T(8,128)S(1)} custom-call(f32[128,128]{1,0:T(8,128)S(1)} %cholesky.267), custom_call_target="Cholesky" | custom-call | tf_op jit(solution)/shard_map/jit(cholesky)/cholesky | solution.py:69
  328.6 9.8 %custom-call.33 = f32[1,128,128]{1,2,0:T(8,128)S(1)} custom-call(f32[1,128,128]{2,1,0:T(8,128)S(1)} %get-tuple-element.83), custom_call_target="InvertDiagBlocksLowerTriangular" | custom-call | tf_op jit(solution)/shard_map/jit(cholesky)/cholesky | solution.py:69
  338.4 0.9 convolution_dynamic-update-slice_fusion
  339.4 1.4 convolution_subtract_fusion.5
  340.8 11.7 %cholesky.236 = f32[128,128]{1,0:T(8,128)S(1)} custom-call(f32[128,128]{1,0:T(8,128)S(1)} %cholesky.272), custom_call_target="Cholesky" | custom-call | tf_op jit(solution)/shard_map/jit(cholesky)/cholesky | solution.py:69
  353.1 9.8 %custom-call.34 = f32[1,128,128]{1,2,0:T(8,128)S(1)} custom-call(f32[1,128,128]{2,1,0:T(8,128)S(1)} %get-tuple-element.80), custom_call_target="InvertDiagBlocksLowerTriangular" | custom-call | tf_op jit(solution)/shard_map/jit(cholesky)/cholesky | solution.py:69
  363.0 0.8 convolution_dynamic-update-slice_fusion.1
  363.8 1.4 convolution_subtract_fusion.6
  365.2 11.9 %cholesky.253 = f32[128,128]{1,0:T(8,128)S(1)} custom-call(f32[128,128]{1,0:T(8,128)S(1)} %convolution_subtract_fusion.6), custom_call_target="Cholesky" | custom-call | tf_op jit(solution)/shard_map/jit(cholesky)/cholesky | solution.py:69
  382.1 2.3 select_select_fusion
  384.4 14.6 %while.12 = (s32[]{:T(128)}, f32[512,512]{1,0:T(8,128)}, s32[4,2]{0,1:T(2,128)S(1)}, f32[4,128,128]{2,1,0:T(8,128)}, s32[]{:T(128)}) while((s32[]{:T(128)}, f32[512,512]{1,0:T(8,128)}, s32[4,2]{0,1:T(2,128)S(1)}, f32[4,128,128]{2,1,0:T(8,128)}, s32[]{:T(128)}) %tuple.52), condition=%wide.while_cond, body=%wide.while_body.sunk | while | flops 2 | bytes 132705 | solution.py:14
  385.1 3.0 bitcast_dynamic-update-slice_fusion.2
  388.7 3.0 bitcast_dynamic-update-slice_fusion.2
  392.4 3.0 bitcast_dynamic-update-slice_fusion.2
  396.1 2.9 bitcast_dynamic-update-slice_fusion.2
  399.0 40.1 %custom-call.35 = f32[4,128,128]{1,2,0:T(8,128)S(1)} custom-call(f32[4,128,128]{2,1,0:T(8,128)} %get-tuple-element.41), custom_call_target="InvertDiagBlocksLowerTriangular" | custom-call | tf_op jit(solution)/shard_map/triangular_solve | solution.py:14
  439.1 28.5 %all-reduce.6.cloned.1.call-done = f32[512,1000]{0,1:T(8,128)} async-done(((f32[512,1000]{0,1:T(8,128)}), f32[512,1000]{0,1:T(8,128)}) %all-reduce.6.cloned.1.call-update) | async-done | bytes 2048016 | tf_op jit(solution)/shard_map/psum | solution.py:66
  467.6 1.9 broadcast_multiply_fusion
  469.5 0.9 fusion.29
  470.5 1.0 convolution_subtract_fusion.3
  471.5 1.0 fusion.53
  472.4 1.0 convolution_subtract_fusion.1
  473.4 0.9 fusion.55
  474.4 1.8 fusion.16
  476.1 1.0 fusion.57
  477.1 1.0 fusion.56
  478.1 1.0 convolution_subtract_fusion.2
  479.0 1.0 fusion.54
  480.0 1.0 convolution_subtract_fusion
  481.0 1.2 fusion.52
  482.2 1.8 fusion.13
  484.0 1.0 fusion.51
  486.4 1.7 add_convert_fusion
  488.2 31.7 %reduce-scatter.2.cloned.1.call-done = bf16[64,1000]{1,0:T(8,128)(2,1)} async-done(((bf16[512,1000]{1,0:T(8,128)(2,1)}), bf16[64,1000]{1,0:T(8,128)(2,1)}) %reduce-scatter.2.cloned.1.call-update) | async-done | bytes 128016 | tf_op jit(solution)/shard_map/reduce_scatter | solution.py:72
  519.8 1.6 convert_subtract_fusion.1
  (67 shorter events, 16.9 us)
Async XLA Ops:
  7.2 32.9 %all-gather.2.cloned.1.call-start = ((), (), s32[]{:S(2)}) async-start(), calls=%async_computation.1 | async-start | bytes 3538944 | tf_op jit(solution)/shard_map/all_gather | solution.py:52
  7.9 274.4 %all-reduce.4.cloned.1.call-start = ((), (), s32[]{:S(2)}) async-start(), calls=%async_computation.2 | async-start | bytes 2097152 | tf_op jit(solution)/shard_map/psum | solution.py:63
  8.7 31.4 %copy-start.5 = (f32[128]{0:T(128)S(1)}, f32[128]{0:T(128)}, u32[]{:S(2)}) copy-start(f32[128]{0:T(128)} %param.11) | copy-start | bytes 1540
  192.4 3.0 copy-start.4
  195.1 2.1 copy-start.1
  195.1 272.5 %all-reduce.6.cloned.1.call-start = ((), (), s32[]{:S(2)}) async-start(), calls=%async_computation.3 | async-start | bytes 4096000 | tf_op jit(solution)/shard_map/psum | solution.py:66
  289.0 1.0 copy-start.3
  377.1 7.3 %copy-start.6 = (s32[4]{0:T(128)S(1)}, s32[4]{0:T(128)}, u32[]{:S(2)}) copy-start(s32[4]{0:T(128)} %iota_multiply_fusion) | copy-start | bytes 52
  377.1 142.7 %reduce-scatter.2.cloned.1.call-start = ((), (), s32[]{:S(2)}) async-start(), calls=%async_computation.4 | async-start | bytes 1179648 | tf_op jit(solution)/shard_map/reduce_scatter | solution.py:72
  467.6 2.8 copy-start.2
  485.1 1.3 copy-start
Sparse Core Ops, SparseCore 0:
  9.7 30.3 all-gather.1
  195.2 86.9 all-reduce.3
  377.2 90.3 all-reduce.5
  488.3 31.4 reduce-scatter.1
where the time goes:
time: 533 us; the launch traced here: 528 us
  other arithmetic  198 us (37%)
  waiting for transfers between devices  171 us (32%)
  matrix products  108 us (20%)
  local copies, waits for them, and re-layouts  34.7 us (7%)
  between operations  16.6 us (3%)
    psum x1, waiting for transfers between devices, shards(): gram = lax.psum(left_product(feats, feats), 'dp')  82 us
    another operation x14, other arithmetic, shards(): factor = jnp.linalg.cholesky(gram)  80.7 us
    conv_general_dilated x4, matrix products, conv_pool(): lax.conv_general_dilated(pics, kernel, (1, 1), 'VALID', dimension_numbers...  76.5 us
    reduce_sum x4, other arithmetic, conv_pool(): response.reshape(count, 2, half, 2, half, filt_count).mean(axis=(2, 4))  64.5 us
    another operation x4, other arithmetic, chol_solve(): lax.linalg.triangular_solve(factor, middle, left_side=True, lower=True, t...  43.1 us
    reduce_scatter x1, waiting for transfers between devices, shards(): lax.psum_scatter((jnp.dot(feats, sol_upper, preferred_element_type=jnp.fl...  31.7 us
    psum x1, waiting for transfers between devices, shards(): cross = lax.psum(cross, 'dp')  28.5 us
    all_gather x1, waiting for transfers between devices, shards(): piece = lax.all_gather(images, 'feat', axis=0, tiled=True)  28 us
  transfers between devices with their start and end apart: 4, of which 4 were waited for; matrix products, arithmetic and copies ran while one was open for 13% of the time, Pallas kernels for 0%

commit v1 on v0

--- a/solution.py
+++ b/solution.py
@@ -63,7 +63,8 @@
     gram = lax.psum(left_product(feats, feats), "dp")
     cross = left_product(feats, res_upper) + left_product(feats, res_lower)
     cross, gram = lax.optimization_barrier((cross, gram))
-    cross = lax.psum(cross, "dp")
+    pieces = lax.all_gather(cross, "dp", axis=0, tiled=False)
+    cross = pieces.sum(axis=0)
     gram = gram / total_images + 0.5 * jnp.eye(width, dtype=jnp.float32)
     cross = cross / total_images
     factor = jnp.linalg.cholesky(gram)

time: 533 us -> 566 us (1.062)
  local copies, waits for them, and re-layouts: 34.7 us -> 49.1 us
  waiting for transfers between devices: 171 us -> 185 us
    all_gather x0 -> x1, waiting for transfers between devices: none -> 41.2 us  [shards(): pieces = lax.all_gather(cross, 'dp', axis=0, tiled=False)]
    psum x1 -> x0, waiting for transfers between devices: 28.5 us -> none  [shards(): cross = lax.psum(cross, 'dp')]
    unnamed x15 -> x14, local copies, waits for them, and re-layouts: 4.41 us -> 21.5 us
    reduce_sum x0 -> x1, other arithmetic: none -> 6.02 us  [shards(): cross = pieces.sum(axis=0)]
  transfers between devices with their start and end apart: 4 -> 4, of which waited for: 4 -> 4; matrix products, arithmetic and copies ran while one was open for 13% -> 28% of each run, Pallas kernels for 0% -> 0%
where the time goes in v1:
time: 566 us; the launch traced here: 560 us
  other arithmetic  201 us (36%)
  waiting for transfers between devices  185 us (33%)
  matrix products  108 us (19%)
  local copies, waits for them, and re-layouts  49.1 us (9%)
  between operations  16.6 us (3%)
    psum x1, waiting for transfers between devices, shards(): gram = lax.psum(left_product(feats, feats), 'dp')  82.1 us
    another operation x14, other arithmetic, shards(): factor = jnp.linalg.cholesky(gram)  80.7 us
    conv_general_dilated x4, matrix products, conv_pool(): lax.conv_general_dilated(pics, kernel, (1, 1), 'VALID', dimension_numbers...  76.5 us
    reduce_sum x4, other arithmetic, conv_pool(): response.reshape(count, 2, half, 2, half, filt_count).mean(axis=(2, 4))  64.5 us
    another operation x4, other arithmetic, chol_solve(): lax.linalg.triangular_solve(factor, middle, left_side=True, lower=True, t...  41.8 us
    all_gather x1, waiting for transfers between devices, shards(): pieces = lax.all_gather(cross, 'dp', axis=0, tiled=False)  41.2 us
    reduce_scatter x1, waiting for transfers between devices, shards(): lax.psum_scatter((jnp.dot(feats, sol_upper, preferred_element_type=jnp.fl...  32.3 us
    all_gather x1, waiting for transfers between devices, shards(): piece = lax.all_gather(images, 'feat', axis=0, tiled=True)  28.5 us
  transfers between devices with their start and end apart: 4, of which 4 were waited for; matrix products, arithmetic and copies ran while one was open for 28% of the time, Pallas kernels for 0%

profile of v1, /device:TPU:0, one launch (start us, length us, event | category | flops | bytes accessed | tf_op | source)
XLA Modules:
  0.0 559.9 jit_solution(5790495208748664000)
XLA Ops:
  8.7 2.9 copy.22
  11.6 28.5 %all-gather.4.cloned.1.call-done = bf16[512,3072]{1,0:T(8,128)(2,1)} async-done(((bf16[64,3072]{1,0:T(8,128)(2,1)}), bf16[512,3072]{1,0:T(8,128)(2,1)}) %all-gather.4.cloned.1.call-update) | async-done | bytes 3145744 | tf_op jit(solution)/shard_map/all_gather | solution.py:52
  40.1 152.3 %while.11 = (s32[]{:T(128)}, bf16[4,128,512]{1,2,0:T(8,128)(2,1)}, bf16[4,128,3072]{2,1,0:T(8,128)(2,1)}, bf16[5,5,3,128]{3,2,1,0:T(4,128)(2,1)S(1)}, f32[128]{0:T(128)S(1)}, /*index=5*/s32[]{:T(128)}, f32[]{:T(128)}) while((s32[]{:T(128)}, bf16[4,128,512]{1,2,0:T(8,128)(2,1)}, bf16[4,128,3072]{2,1,0:T(8,128)(2,1)}, ...), condition=%wide.region_2.3_spmd, body=%wide.region_0.2_spmd.sunk | while | flops 1965359104 | bytes 109464928 | solution.py:56
  40.1 1.2 constant_dynamic-slice_fusion.4
  42.1 19.1 %add_maximum_fusion.2 = f32[128,28,28,128]{3,0,2,1:T(8,128)} fusion(f32[128]{0:T(128)S(1)} %get-tuple-element.169, bf16[128,32,32,3]{0,3,2,1:T(4,128)(2,1)S(1)} %reshape.102, bf16[5,5,3,128]{3,2,1,0:T(4,128)(2,1)S(1)} %get-tuple-element.168), kind=kOutput, calls=%fused_computation.clone.1 | convolution fusion | flops 1952448512 | bytes 52186368 | tf_op jit(solution)/shard_map/while/body/eval_jaxpr/conv_general_dilated | solution.py:33
  61.2 16.1 %reduce_sum.21 = f32[128,2,2,128]{3,0,2,1:T(8,128)S(1)} reduce(f32[128,2,14,2,14,128]{5,0,4,3,2,1:T(8,128)} %bitcast.90, f32[]{:T(128)} %constant.174.clone.1..sunk), dimensions={2,4}, to_apply=%region_1.1 | reduce | flops 12779520 | bytes 51642372 | tf_op jit(solution)/shard_map/while/body/eval_jaxpr/reduce_sum | solution.py:43
  78.2 1.2 constant_dynamic-slice_fusion.4
  80.1 19.1 %add_maximum_fusion.2 = f32[128,28,28,128]{3,0,2,1:T(8,128)} fusion(f32[128]{0:T(128)S(1)} %get-tuple-element.169, bf16[128,32,32,3]{0,3,2,1:T(4,128)(2,1)S(1)} %reshape.102, bf16[5,5,3,128]{3,2,1,0:T(4,128)(2,1)S(1)} %get-tuple-element.168), kind=kOutput, calls=%fused_computation.clone.1 | convolution fusion | flops 1952448512 | bytes 52186368 | tf_op jit(solution)/shard_map/while/body/eval_jaxpr/conv_general_dilated | solution.py:33
  99.3 16.1 %reduce_sum.21 = f32[128,2,2,128]{3,0,2,1:T(8,128)S(1)} reduce(f32[128,2,14,2,14,128]{5,0,4,3,2,1:T(8,128)} %bitcast.90, f32[]{:T(128)} %constant.174.clone.1..sunk), dimensions={2,4}, to_apply=%region_1.1 | reduce | flops 12779520 | bytes 51642372 | tf_op jit(solution)/shard_map/while/body/eval_jaxpr/reduce_sum | solution.py:43
  116.2 1.2 constant_dynamic-slice_fusion.4
  118.2 19.1 %add_maximum_fusion.2 = f32[128,28,28,128]{3,0,2,1:T(8,128)} fusion(f32[128]{0:T(128)S(1)} %get-tuple-element.169, bf16[128,32,32,3]{0,3,2,1:T(4,128)(2,1)S(1)} %reshape.102, bf16[5,5,3,128]{3,2,1,0:T(4,128)(2,1)S(1)} %get-tuple-element.168), kind=kOutput, calls=%fused_computation.clone.1 | convolution fusion | flops 1952448512 | bytes 52186368 | tf_op jit(solution)/shard_map/while/body/eval_jaxpr/conv_general_dilated | solution.py:33
  137.3 16.1 %reduce_sum.21 = f32[128,2,2,128]{3,0,2,1:T(8,128)S(1)} reduce(f32[128,2,14,2,14,128]{5,0,4,3,2,1:T(8,128)} %bitcast.90, f32[]{:T(128)} %constant.174.clone.1..sunk), dimensions={2,4}, to_apply=%region_1.1 | reduce | flops 12779520 | bytes 51642372 | tf_op jit(solution)/shard_map/while/body/eval_jaxpr/reduce_sum | solution.py:43
  154.3 1.2 constant_dynamic-slice_fusion.4
  156.3 19.1 %add_maximum_fusion.2 = f32[128,28,28,128]{3,0,2,1:T(8,128)} fusion(f32[128]{0:T(128)S(1)} %get-tuple-element.169, bf16[128,32,32,3]{0,3,2,1:T(4,128)(2,1)S(1)} %reshape.102, bf16[5,5,3,128]{3,2,1,0:T(4,128)(2,1)S(1)} %get-tuple-element.168), kind=kOutput, calls=%fused_computation.clone.1 | convolution fusion | flops 1952448512 | bytes 52186368 | tf_op jit(solution)/shard_map/while/body/eval_jaxpr/conv_general_dilated | solution.py:33
  175.4 16.1 %reduce_sum.21 = f32[128,2,2,128]{3,0,2,1:T(8,128)S(1)} reduce(f32[128,2,14,2,14,128]{5,0,4,3,2,1:T(8,128)} %bitcast.90, f32[]{:T(128)} %constant.174.clone.1..sunk), dimensions={2,4}, to_apply=%region_1.1 | reduce | flops 12779520 | bytes 51642372 | tf_op jit(solution)/shard_map/while/body/eval_jaxpr/reduce_sum | solution.py:43
  192.4 2.7 convolution_bitcast_fusion
  195.1 1.9 convert_subtract_fusion
  198.0 2.0 convolution_add_fusion
  200.1 82.1 %all-reduce.3.cloned.1.call-done = f32[512,512]{1,0:T(8,128)} async-done(((f32[512,512]{1,0:T(8,128)}), f32[512,512]{1,0:T(8,128)}) %all-reduce.3.cloned.1.call-update) | async-done | bytes 1048592 | tf_op jit(solution)/shard_map/psum | solution.py:63
  282.5 2.3 select_add_fusion
  284.8 2.6 copy.24
  287.4 1.8 fusion.19
  289.2 1.0 copy-done.3
  290.1 11.7 %cholesky.103 = f32[128,128]{1,0:T(8,128)S(1)} custom-call(f32[128,128]{1,0:T(8,128)S(1)} %cholesky.263), custom_call_target="Cholesky" | custom-call | tf_op jit(solution)/shard_map/jit(cholesky)/cholesky | solution.py:70
  301.9 1.1 cholesky.222
  303.0 9.8 %custom-call.32 = f32[1,128,128]{1,2,0:T(8,128)S(1)} custom-call(f32[1,128,128]{2,1,0:T(8,128)S(1)} %get-tuple-element.86), custom_call_target="InvertDiagBlocksLowerTriangular" | custom-call | tf_op jit(solution)/shard_map/jit(cholesky)/cholesky | solution.py:70
  312.8 2.0 constant_dynamic-update-slice_fusion.4
  314.8 1.3 convolution_subtract_fusion.4
  316.1 11.7 %cholesky.215 = f32[128,128]{1,0:T(8,128)S(1)} custom-call(f32[128,128]{1,0:T(8,128)S(1)} %cholesky.267), custom_call_target="Cholesky" | custom-call | tf_op jit(solution)/shard_map/jit(cholesky)/cholesky | solution.py:70
  328.4 10.2 %custom-call.33 = f32[1,128,128]{1,2,0:T(8,128)S(1)} custom-call(f32[1,128,128]{2,1,0:T(8,128)S(1)} %get-tuple-element.83), custom_call_target="InvertDiagBlocksLowerTriangular" | custom-call | tf_op jit(solution)/shard_map/jit(cholesky)/cholesky | solution.py:70
  338.6 0.9 convolution_dynamic-update-slice_fusion
  339.5 1.4 convolution_subtract_fusion.5
  341.0 11.7 %cholesky.236 = f32[128,128]{1,0:T(8,128)S(1)} custom-call(f32[128,128]{1,0:T(8,128)S(1)} %cholesky.272), custom_call_target="Cholesky" | custom-call | tf_op jit(solution)/shard_map/jit(cholesky)/cholesky | solution.py:70
  353.4 9.8 %custom-call.34 = f32[1,128,128]{1,2,0:T(8,128)S(1)} custom-call(f32[1,128,128]{2,1,0:T(8,128)S(1)} %get-tuple-element.80), custom_call_target="InvertDiagBlocksLowerTriangular" | custom-call | tf_op jit(solution)/shard_map/jit(cholesky)/cholesky | solution.py:70
  363.2 0.9 convolution_dynamic-update-slice_fusion.1
  364.0 1.4 convolution_subtract_fusion.6
  365.4 11.7 %cholesky.253 = f32[128,128]{1,0:T(8,128)S(1)} custom-call(f32[128,128]{1,0:T(8,128)S(1)} %convolution_subtract_fusion.6), custom_call_target="Cholesky" | custom-call | tf_op jit(solution)/shard_map/jit(cholesky)/cholesky | solution.py:70
  382.2 2.4 select_select_fusion
  384.6 12.0 %while.12 = (s32[]{:T(128)}, f32[512,512]{1,0:T(8,128)}, s32[4,2]{0,1:T(2,128)S(1)}, f32[4,128,128]{2,1,0:T(8,128)S(1)}, s32[]{:T(128)}) while((s32[]{:T(128)}, f32[512,512]{1,0:T(8,128)}, s32[4,2]{0,1:T(2,128)S(1)}, f32[4,128,128]{2,1,0:T(8,128)S(1)}, s32[]{:T(128)}) %tuple.52), condition=%wide.while_cond, body=%wide.while_body.sunk | while | flops 2 | bytes 131189 | solution.py:14
  385.3 2.3 bitcast_dynamic-update-slice_fusion.2
  388.3 2.3 bitcast_dynamic-update-slice_fusion.2
  391.3 2.3 bitcast_dynamic-update-slice_fusion.2
  394.3 2.3 bitcast_dynamic-update-slice_fusion.2
  396.6 39.3 %custom-call.35 = f32[4,128,128]{1,2,0:T(8,128)S(1)} custom-call(f32[4,128,128]{2,1,0:T(8,128)S(1)} %get-tuple-element.41), custom_call_target="InvertDiagBlocksLowerTriangular" | custom-call | tf_op jit(solution)/shard_map/triangular_solve | solution.py:14
  435.9 41.2 %all-gather.6.cloned.1.call-done = f32[8192,1000]{0,1:T(8,128)} async-done(((f32[512,1000]{0,1:T(8,128)}), f32[8192,1000]{0,1:T(8,128)}) %all-gather.6.cloned.1.call-update) | async-done | bytes 32768016 | tf_op jit(solution)/shard_map/all_gather | solution.py:66
  477.1 17.1 %copy.27 = f32[125,8,16,512]{3,2,1,0:T(8,128)S(1)} copy(f32[125,8,16,512]{3,1,2,0:T(8,128)} %bitcast.91) | data formatting | bytes 65536000
  494.2 6.0 %bitcast_reduce_fusion = f32[512,1000]{0,1:T(8,128)S(1)} fusion(f32[125,8,16,512]{3,2,1,0:T(8,128)S(1)} %copy.27), kind=kLoop, calls=%fused_computation.7 | loop fusion | flops 7680000 | bytes 34816000 | tf_op jit(solution)/shard_map/reduce_sum | solution.py:67
  500.5 1.0 fusion.29
  501.5 1.0 convolution_subtract_fusion.3
  502.5 1.0 fusion.53
  503.4 1.0 convolution_subtract_fusion.1
  504.4 0.9 fusion.55
  505.4 1.8 fusion.16
  507.1 0.9 fusion.57
  508.1 1.0 fusion.56
  509.1 1.0 convolution_subtract_fusion.2
  510.0 1.0 fusion.54
  511.0 1.0 convolution_subtract_fusion
  512.0 1.2 fusion.52
  513.2 1.8 fusion.13
  515.0 1.0 fusion.51
  517.4 1.7 add_convert_fusion
  519.2 32.3 %reduce-scatter.2.cloned.1.call-done = bf16[64,1000]{1,0:T(8,128)(2,1)} async-done(((bf16[512,1000]{1,0:T(8,128)(2,1)}), bf16[64,1000]{1,0:T(8,128)(2,1)}) %reduce-scatter.2.cloned.1.call-update) | async-done | bytes 128016 | tf_op jit(solution)/shard_map/reduce_scatter | solution.py:73
  551.5 1.6 convert_subtract_fusion.1
  (67 shorter events, 17.6 us)
Async XLA Ops:
  7.2 32.9 %all-gather.4.cloned.1.call-start = ((), (), s32[]{:S(2)}) async-start(), calls=%async_computation.1 | async-start | bytes 3538944 | tf_op jit(solution)/shard_map/all_gather | solution.py:52
  7.9 274.3 %all-reduce.3.cloned.1.call-start = ((), (), s32[]{:S(2)}) async-start(), calls=%async_computation.2 | async-start | bytes 2097152 | tf_op jit(solution)/shard_map/psum | solution.py:63
  8.7 31.4 %copy-start.5 = (f32[128]{0:T(128)S(1)}, f32[128]{0:T(128)}, u32[]{:S(2)}) copy-start(f32[128]{0:T(128)} %param.11) | copy-start | bytes 1540
  192.4 2.8 copy-start.4
  195.1 2.0 copy-start.1
  195.1 282.0 %all-gather.6.cloned.1.call-start = ((), (), s32[]{:S(2)}) async-start(), calls=%async_computation.4 | async-start | bytes 34816000 | tf_op jit(solution)/shard_map/all_gather | solution.py:66
  282.2 269.2 %reduce-scatter.2.cloned.1.call-start = ((), (), s32[]{:S(2)}) async-start(), calls=%async_computation.3 | async-start | bytes 1179648 | tf_op jit(solution)/shard_map/reduce_scatter | solution.py:73
  289.1 1.0 copy-start.3
  500.2 1.2 copy-start.2
  516.1 1.3 copy-start
Sparse Core Ops, SparseCore 0:
  9.7 30.3 all-gather.3
  195.2 86.9 all-reduce.2
  285.0 192.0 all-gather.5
  519.3 32.1 reduce-scatter.1
